TPU v7x, 128 devices: a whole 4x4x4 slice. The times are simulated.
128 devices in a mesh: row: 8 (over y, core), col: 16 (over z, x).
Axes of the slice: x: 4, y: 4, z: 4, core: 2. Of those that a mesh axis runs over, the one named last changes fastest.
Arguments:
- fock: bfloat16 [32768, 16, 2048], P('row', 'col'), may hold values from -6 to 6
- lmo_coef: bfloat16 [32768, 1024], P(('row', 'col')), may hold values from -0.078125 to 0.078125
- three_index: bfloat16 [32768, 512], P(('row', 'col')), may hold values from -6 to 6
- rotation: bfloat16 [16, 8, 1024, 512], P('col', 'row'), may hold values from -0.1875 to 0.1875
- lmo_ids: int32 [16, 8], replicated, may hold values from 0 to 127, as said below
- domains: int32 [128, 8], replicated, may hold values from -1 to 255, as said below
Outputs:
- proj_fock: float32 [16, 8, 512, 512], P('col', 'row')
- three_rot: bfloat16 [16, 8, 512, 512], P('col', 'row')
Inputs may be any that keep to these rules, and one draw needn't show every extreme that they name: `lmo_ids`: every LMO number appears exactly once; row o lists the 8 LMOs owned by column set o. `domains`: entry k of a list is -1 or a block of row panel k; entry 0 is never -1. The present blocks of one list lie in distinct column sets. For one owner o and one entry k, the blocks of the lists of lmo_ids[o, j] over all j lie in distinct column sets; for one j and one entry k, those of lmo_ids[o, j] over all o do too.
All inputs are finite; a program needn't handle non-finite values.
Results may differ from a plain program's by a relative error of at most 0.02.
Values may be sent and summed in bfloat16 or wider, within the bound.
No kernel may reach another device: no remote copies, remote signals or barrier semaphores. Data moves between devices by JAX's collectives and lax.ppermute only.
A program may use at most 192 MiB of HBM per device.

v0:
```python
import jax
import jax.numpy as jnp
from jax import lax
from jax.sharding import PartitionSpec as P

BLK = 128
F32 = jnp.float32
BF16 = jnp.bfloat16


def pick(mask, table):
    return jnp.sum(jnp.where(mask, table, 0), axis=-1)


def body(fock, lmo_coef, three_index, rotation, lmo_ids, domains):
    num_sets = lax.axis_size("col")
    my_row = lax.axis_index("row")
    my_col = lax.axis_index("col")
    dev_rows = lmo_coef.shape[0]
    occ_width = lmo_coef.shape[1]
    dev_blocks = dev_rows // BLK
    dom_blocks = domains.shape[1]
    dom_width = dom_blocks * BLK
    panel_fock = fock[:, 0, :]
    panel_blocks = panel_fock.shape[0] // BLK
    col_blocks = panel_fock.shape[1] // BLK
    doms = jnp.take(domains, lmo_ids, axis=0)
    present = doms >= 0
    clipped = jnp.maximum(doms, 0)
    flat = clipped // dev_blocks
    cset = flat % num_sets
    sub = clipped % dev_blocks
    panel = flat // num_sets
    row_tile = cset * dev_blocks + sub
    col_tile = panel * dev_blocks + sub
    pres_k = lax.dynamic_index_in_dim(present, my_row, 2, keepdims=False)
    cset_k = lax.dynamic_index_in_dim(cset, my_row, 2, keepdims=False)
    sub_k = lax.dynamic_index_in_dim(sub, my_row, 2, keepdims=False)
    rtile_k = lax.dynamic_index_in_dim(row_tile, my_row, 2, keepdims=False)
    mine_k = pres_k & (cset_k == my_col)
    sub_o = pick(mine_k, sub_k)
    mine2 = present & (cset == my_col)
    ct = pick(mine2, col_tile)
    fock_tiles = panel_fock.reshape(panel_blocks, BLK, col_blocks, BLK)
    tiles_a = fock_tiles.at[rtile_k, :, ct, :].get(mode="promise_in_bounds")
    in_rows = jnp.concatenate([lmo_coef, three_index], axis=1).reshape(dev_blocks, BLK, -1)
    rows_a = jnp.take(in_rows, sub_o, axis=0, mode="clip")
    rows_a = lax.all_to_all(rows_a, "col", 0, 0, tiled=True)
    tiles_a, rows_a = lax.optimization_barrier((tiles_a, rows_a))
    tiles_a = lax.all_to_all(tiles_a, "col", 0, 0, tiled=True)
    gathered = lax.all_gather(lmo_coef, "row", axis=0, tiled=True)
    fock_lmo = jnp.dot(panel_fock, gathered, preferred_element_type=F32).astype(BF16)
    rows_a, tiles_a, fock_lmo = lax.optimization_barrier((rows_a, tiles_a, fock_lmo))
    coef_b = lax.psum_scatter(fock_lmo, "col", scatter_dimension=0, tiled=True)
    occ_term = jnp.einsum("ri,rj->ij", lmo_coef, coef_b, preferred_element_type=F32)
    occ_b = lax.psum(occ_term, ("row", "col")).astype(BF16)
    pres_o = lax.dynamic_index_in_dim(present, my_col, 0, keepdims=False)
    cset_o = lax.dynamic_index_in_dim(cset, my_col, 0, keepdims=False)
    pres_jk = lax.dynamic_index_in_dim(pres_o, my_row, 1, keepdims=False)
    cset_jk = lax.dynamic_index_in_dim(cset_o, my_row, 1, keepdims=False)
    rows_b = jnp.take(rows_a, cset_jk, axis=0, mode="clip")
    rows_b = jnp.where(pres_jk[:, None, None], rows_b, jnp.zeros_like(rows_b))
    slot_ids = jnp.broadcast_to(jnp.arange(dom_blocks, dtype=jnp.int32)[:, None], cset_o.shape)
    tiles_b = tiles_a.at[cset_o, slot_ids].get(mode="promise_in_bounds")
    live_b = pres_o & pres_jk[:, None]
    tiles_b = jnp.where(live_b[:, :, None, None], tiles_b, jnp.zeros_like(tiles_b))
    rows_dom, tiles_dom = (
        lax.all_to_all(rows_b, "row", 0, 0, tiled=True),
        lax.all_to_all(tiles_b, "row", 0, 0, tiled=True),
    )
    rows_dom = rows_dom.reshape(dom_width, -1)
    fc_a = jnp.take(coef_b.reshape(dev_blocks, BLK, occ_width), sub_o, axis=0, mode="clip")
    fc_a = lax.all_to_all(fc_a, "col", 0, 0, tiled=True)
    fc_a, occ_b, rows_dom, tiles_dom = lax.optimization_barrier((fc_a, occ_b, rows_dom, tiles_dom))
    fc_b = jnp.take(fc_a, cset_jk, axis=0, mode="clip")
    fc_b = jnp.where(pres_jk[:, None, None], fc_b, jnp.zeros_like(fc_b))
    fc_dom = lax.all_to_all(fc_b, "row", 0, 0, tiled=True).reshape(dom_width, occ_width)
    coef_dom = rows_dom[:, :occ_width]
    three_dom = rows_dom[:, occ_width:]
    correction = jnp.dot(coef_dom, occ_b, preferred_element_type=F32)
    proj_dom = (fc_dom.astype(F32) - 0.5 * correction).astype(BF16)
    slot_rot = rotation[0, 0]
    rot_tiles = slot_rot.reshape(dom_blocks, BLK, -1)
    fock_half = jnp.einsum("abtu,bun->atn", tiles_dom, rot_tiles, preferred_element_type=F32)
    fock_half = fock_half.reshape(dom_width, -1).astype(BF16)
    fock_rot = jnp.einsum("xm,xn->mn", slot_rot, fock_half, preferred_element_type=F32)
    coef_rot = jnp.einsum("xm,xi->mi", slot_rot, coef_dom, preferred_element_type=F32).astype(BF16)
    proj_rot = jnp.einsum("xm,xi->mi", slot_rot, proj_dom, preferred_element_type=F32).astype(BF16)
    proj_fock = fock_rot - jnp.einsum("mi,ni->mn", coef_rot, proj_rot, preferred_element_type=F32)
    proj_fock = proj_fock - jnp.einsum("mi,ni->mn", proj_rot, coef_rot, preferred_element_type=F32)
    three_rot = jnp.einsum("xm,xu->mu", slot_rot, three_dom, preferred_element_type=F32).astype(
        BF16
    )
    return (proj_fock[None, None], three_rot[None, None])


def solution(mesh):
    placed = (
        P("row", "col", None),
        P(("row", "col"), None),
        P(("row", "col"), None),
        P("col", "row", None, None),
        P(),
        P(),
    )
    return jax.shard_map(
        body,
        mesh=mesh,
        in_specs=placed,
        out_specs=(P("col", "row", None, None), P("col", "row", None, None)),
        check_vma=False,
    )
```

profile of v0, /device:TPU:1, one launch (start us, length us, event | category | flops | bytes accessed | tf_op | source)
XLA Modules:
  0.0 483.2 jit_solution(15179841917422128813)
XLA Ops:
  12.3 3.6 gather_fusion.2
  15.9 8.5 %all-to-all-start = ((bf16[16,128,1536]{2,1,0:T(8,128)(2,1)}), bf16[16,128,1536]{2,1,0:T(8,128)(2,1)}, u32[]{:S(2)}, u32[]{:S(2)}) async-start(bf16[16,128,1536]{2,1,0:T(8,128)(2,1)} %gather_fusion.2), calls=%async_computation | async-start | bytes 12582912 | tf_op jit(solution)/shard_map/all_to_all | solution.py:48
  24.4 9.7 %copy.44 = bf16[512,8,16,128]{3,2,1,0:T(8,128)(2,1)S(1)} copy(bf16[512,8,16,128]{3,1,2,0:T(8,128)(2,1)} %bitcast.68) | data formatting | bytes 33554432
  34.1 8.2 %copy.33 = bf16[32,128,16,128]{3,1,2,0:T(8,128)(2,1)} copy(bf16[32,128,16,128]{3,2,1,0:T(8,128)(2,1)S(1)} %bitcast.65) | data formatting | bytes 33554432 | tf_op jit(solution)/shard_map/reshape;squeeze | solution.py:44
  42.5 9.0 %gather_fusion.1 = bf16[128,128,128]{2,1,0:T(8,128)(2,1)} fusion(bf16[32,128,16,128]{3,1,2,0:T(8,128)(2,1)} %copy.33, s32[128]{0:T(128)S(1)} %reshape.121), kind=kCustom, calls=%fused_computation.1 | custom fusion | bytes 8389632 | tf_op jit(solution)/shard_map/gather | solution.py:45
  51.5 65.2 %all-to-all-done = bf16[16,128,1536]{2,1,0:T(8,128)(2,1)} async-done(((bf16[16,128,1536]{2,1,0:T(8,128)(2,1)}), bf16[16,128,1536]{2,1,0:T(8,128)(2,1)}, u32[]{:S(2)}, u32[]{:S(2)}) %all-to-all-start) | async-done | bytes 6291488 | tf_op jit(solution)/shard_map/all_to_all | solution.py:48
  116.7 5.4 %all-to-all-start.1 = ((bf16[16,8,128,128]{3,2,1,0:T(8,128)(2,1)}), bf16[16,8,128,128]{3,2,1,0:T(8,128)(2,1)}, u32[]{:S(2)}, u32[]{:S(2)}) async-start(bf16[16,8,128,128]{3,2,1,0:T(8,128)(2,1)} %bitcast.69), calls=%async_computation.1 | async-start | bytes 8388608 | tf_op jit(solution)/shard_map/all_to_all | solution.py:50
  122.2 23.4 %fusion.2 = bf16[4096,1024]{1,0:T(8,128)(2,1)} fusion(bf16[2048,1024]{1,0:T(8,128)(2,1)} %all-gather.2.cloned.1.call-done, bf16[4096,1,2048]{2,0,1:T(8,128)(2,1)} %param.6), kind=kOutput, calls=%fused_computation.9 | convolution fusion | flops 17184063488 | bytes 29360128 | tf_op jit(solution)/shard_map/dot_general | solution.py:52
  145.7 35.7 %all-to-all-done.1 = bf16[16,8,128,128]{3,2,1,0:T(8,128)(2,1)} async-done(((bf16[16,8,128,128]{3,2,1,0:T(8,128)(2,1)}), bf16[16,8,128,128]{3,2,1,0:T(8,128)(2,1)}, u32[]{:S(2)}, u32[]{:S(2)}) %all-to-all-start.1) | async-done | bytes 4194336 | tf_op jit(solution)/shard_map/all_to_all | solution.py:50
  182.2 3.2 gather_fusion.5
  185.4 2.8 copy_select_fusion
  188.2 7.4 %all-to-all-start.4 = ((bf16[8,8,128,128]{3,1,2,0:T(8,128)(2,1)}), bf16[8,8,128,128]{3,1,2,0:T(8,128)(2,1)S(1)}, u32[]{:S(2)}, u32[]{:S(2)}) async-start(bf16[8,8,128,128]{3,1,2,0:T(8,128)(2,1)} %copy_select_fusion), calls=%async_computation.5 | async-start | bytes 4194304 | tf_op jit(solution)/shard_map/all_to_all | solution.py:69
  195.8 5.4 %gather_fusion.4 = bf16[8,128,1536]{2,1,0:T(8,128)(2,1)} fusion(bf16[16,128,1536]{2,1,0:T(8,128)(2,1)} %all-to-all-done, s32[1024]{0:T(1024)S(1)} %pad_clamp_fusion), kind=kCustom, calls=%fused_computation.4 | custom fusion | bytes 6291488 | tf_op jit(solution)/shard_map/jit(_take)/gather | solution.py:61
  201.2 4.0 broadcast_select_fusion
  205.1 16.8 %all-to-all-done.4 = bf16[8,8,128,128]{3,1,2,0:T(8,128)(2,1)S(1)} async-done(((bf16[8,8,128,128]{3,1,2,0:T(8,128)(2,1)}), bf16[8,8,128,128]{3,1,2,0:T(8,128)(2,1)S(1)}, u32[]{:S(2)}, u32[]{:S(2)}) %all-to-all-start.4) | async-done | bytes 2097184 | tf_op jit(solution)/shard_map/all_to_all | solution.py:69
  223.2 5.2 %all-to-all-start.3 = ((bf16[8,128,1536]{2,1,0:T(8,128)(2,1)}), bf16[8,128,1536]{2,1,0:T(8,128)(2,1)}, u32[]{:S(2)}, u32[]{:S(2)}) async-start(bf16[8,128,1536]{2,1,0:T(8,128)(2,1)} %broadcast_select_fusion), calls=%async_computation.4 | async-start | bytes 6291456 | tf_op jit(solution)/shard_map/all_to_all | solution.py:68
  228.4 37.5 %reduce-scatter.2.cloned.1.call-done = bf16[256,1024]{1,0:T(8,128)(2,1)} async-done(((bf16[4096,1024]{1,0:T(8,128)(2,1)}), bf16[256,1024]{1,0:T(8,128)(2,1)}) %reduce-scatter.2.cloned.1.call-update) | async-done | bytes 524304 | tf_op jit(solution)/shard_map/reduce_scatter | solution.py:54
  266.0 3.8 gather_fusion.3
  269.8 4.9 %all-to-all-start.2 = ((bf16[16,128,1024]{2,1,0:T(8,128)(2,1)}), bf16[16,128,1024]{2,1,0:T(8,128)(2,1)}, u32[]{:S(2)}, u32[]{:S(2)}) async-start(bf16[16,128,1024]{2,1,0:T(8,128)(2,1)} %gather_fusion.3), calls=%async_computation.3 | async-start | bytes 8388608 | tf_op jit(solution)/shard_map/all_to_all | solution.py:73
  274.7 2.7 convolution_bitcast_fusion
  277.4 148.5 %all-reduce.1 = bf16[1024,1024]{0,1:T(8,128)(2,1)} all-reduce(f32[1024,1024]{0,1:T(8,128)} %convolution_bitcast_fusion), channel_id=1, replica_groups=mesh['row'=8,'col'=16] {'row','col'}, use_global_device_ids=true, to_apply=%region_3.4 | all-reduce | flops 1048576 | bytes 6291456 | tf_op jit(solution)/shard_map/psum | solution.py:56
  425.9 2.9 gather_fusion.6
  428.8 1.5 broadcast_select_fusion.1
  430.3 7.0 %all-to-all-start.5 = ((bf16[8,128,1024]{2,1,0:T(8,128)(2,1)}), bf16[8,128,1024]{2,1,0:T(8,128)(2,1)}, u32[]{:S(2)}, u32[]{:S(2)}) async-start(bf16[8,128,1024]{2,1,0:T(8,128)(2,1)} %broadcast_select_fusion.1), calls=%async_computation.6 | async-start | bytes 4194304 | tf_op jit(solution)/shard_map/all_to_all | solution.py:77
  437.4 2.0 fusion.17
  440.3 2.9 fusion.11
  443.2 4.3 convolution_bitcast_fusion.1
  447.6 16.3 %all-to-all-done.5 = bf16[8,128,1024]{2,1,0:T(8,128)(2,1)} async-done(((bf16[8,128,1024]{2,1,0:T(8,128)(2,1)}), bf16[8,128,1024]{2,1,0:T(8,128)(2,1)}, u32[]{:S(2)}, u32[]{:S(2)}) %all-to-all-start.5) | async-done | bytes 2097184 | tf_op jit(solution)/shard_map/all_to_all | solution.py:77
  463.8 6.3 %convolution_convert_fusion = bf16[1024,512]{1,0:T(8,128)(2,1)S(1)} fusion(bf16[1,1,1024,512]{3,2,1,0:T(8,128)(2,1)S(1)} %copy-done, bf16[1024,1024]{1,0:T(8,128)(2,1)} %bitcast.22, bf16[1024,1024]{0,1:T(8,128)(2,1)} %all-reduce.1, bf16[1024,1536]{1,0:T(8,128)(2,1)} %bitcast.7), kind=kOutput, calls=%fused_computation.23 | convolution fusion | flops 3225944064 | bytes 8388608 | tf_op jit(solution)/shard_map/xm,xi->mi/dot_general | solution.py:88
  471.1 2.0 convolution_subtract_fusion.1
  473.1 2.0 fusion.16
  475.1 1.3 copy.40
  (43 shorter events, 9.6 us)
Async XLA Ops:
  7.2 430.2 %copy-start = (bf16[1,1,1024,512]{3,2,1,0:T(8,128)(2,1)S(1)}, bf16[1,1,1024,512]{3,2,1,0:T(8,128)(2,1)}, u32[]{:S(2)}) copy-start(bf16[1,1,1024,512]{3,2,1,0:T(8,128)(2,1)} %param.9) | copy-start | bytes 3145732
  7.2 115.0 %all-gather.2.cloned.1.call-start = ((), (), s32[]{:S(2)}) async-start(), calls=%async_computation.7 | async-start | bytes 4718592 | tf_op jit(solution)/shard_map/all_gather | solution.py:51
  15.9 100.8 %all-to-all-start = ((bf16[16,128,1536]{2,1,0:T(8,128)(2,1)}), bf16[16,128,1536]{2,1,0:T(8,128)(2,1)}, u32[]{:S(2)}, u32[]{:S(2)}) async-start(bf16[16,128,1536]{2,1,0:T(8,128)(2,1)} %gather_fusion.2), calls=%async_computation | async-start | bytes 12582912 | tf_op jit(solution)/shard_map/all_to_all | solution.py:48
  116.7 64.7 %all-to-all-start.1 = ((bf16[16,8,128,128]{3,2,1,0:T(8,128)(2,1)}), bf16[16,8,128,128]{3,2,1,0:T(8,128)(2,1)}, u32[]{:S(2)}, u32[]{:S(2)}) async-start(bf16[16,8,128,128]{3,2,1,0:T(8,128)(2,1)} %bitcast.69), calls=%async_computation.1 | async-start | bytes 8388608 | tf_op jit(solution)/shard_map/all_to_all | solution.py:50
  122.1 143.8 %reduce-scatter.2.cloned.1.call-start = ((), (), s32[]{:S(2)}) async-start(), calls=%async_computation.8 | async-start | bytes 8912896 | tf_op jit(solution)/shard_map/reduce_scatter | solution.py:54
  188.2 33.8 %all-to-all-start.4 = ((bf16[8,8,128,128]{3,1,2,0:T(8,128)(2,1)}), bf16[8,8,128,128]{3,1,2,0:T(8,128)(2,1)S(1)}, u32[]{:S(2)}, u32[]{:S(2)}) async-start(bf16[8,8,128,128]{3,1,2,0:T(8,128)(2,1)} %copy_select_fusion), calls=%async_computation.5 | async-start | bytes 4194304 | tf_op jit(solution)/shard_map/all_to_all | solution.py:69
  221.9 1.3 copy-start.4
  223.2 46.6 %all-to-all-start.3 = ((bf16[8,128,1536]{2,1,0:T(8,128)(2,1)}), bf16[8,128,1536]{2,1,0:T(8,128)(2,1)}, u32[]{:S(2)}, u32[]{:S(2)}) async-start(bf16[8,128,1536]{2,1,0:T(8,128)(2,1)} %broadcast_select_fusion), calls=%async_computation.4 | async-start | bytes 6291456 | tf_op jit(solution)/shard_map/all_to_all | solution.py:68
  269.8 4.9 %copy-start.1 = (bf16[256,1024]{1,0:T(8,128)(2,1)S(1)}, bf16[256,1024]{1,0:T(8,128)(2,1)}, u32[]{:S(2)}) copy-start(bf16[256,1024]{1,0:T(8,128)(2,1)} %reduce-scatter.2.cloned.1.call-done) | copy-start | bytes 1572868
  269.8 4.9 %copy-start.2 = (bf16[256,1024]{1,0:T(8,128)(2,1)S(1)}, bf16[256,1024]{1,0:T(8,128)(2,1)}, u32[]{:S(2)}) copy-start(bf16[256,1024]{1,0:T(8,128)(2,1)} %param.7) | copy-start | bytes 1572868
  269.8 156.2 %all-to-all-start.2 = ((bf16[16,128,1024]{2,1,0:T(8,128)(2,1)}), bf16[16,128,1024]{2,1,0:T(8,128)(2,1)}, u32[]{:S(2)}, u32[]{:S(2)}) async-start(bf16[16,128,1024]{2,1,0:T(8,128)(2,1)} %gather_fusion.3), calls=%async_computation.3 | async-start | bytes 8388608 | tf_op jit(solution)/shard_map/all_to_all | solution.py:73
  430.3 33.5 %all-to-all-start.5 = ((bf16[8,128,1024]{2,1,0:T(8,128)(2,1)}), bf16[8,128,1024]{2,1,0:T(8,128)(2,1)}, u32[]{:S(2)}, u32[]{:S(2)}) async-start(bf16[8,128,1024]{2,1,0:T(8,128)(2,1)} %broadcast_select_fusion.1), calls=%async_computation.6 | async-start | bytes 4194304 | tf_op jit(solution)/shard_map/all_to_all | solution.py:77
  470.1 1.0 copy-start.3
Sparse Core Ops, SparseCore 0:
  9.7 35.7 all-gather.1
  181.5 84.3 reduce-scatter.1
where the time goes:
time: 484 us; the launch traced here: 483 us
  waiting for transfers between devices  172 us (36%)
  blocking collectives  149 us (31%)
  local copies, waits for them, and re-layouts  53 us (11%)
  matrix products  45.6 us (9%)
  starting transfers between devices  38.6 us (8%)
  between operations  14.2 us (3%)
  other arithmetic  11 us (2%)
    psum x1, blocking collectives, body(): occ_b = lax.psum(occ_term, ('row', 'col')).astype(BF16)  149 us
    all_to_all x1, waiting for transfers between devices, body(): rows_a = lax.all_to_all(rows_a, 'col', 0, 0, tiled=True)  65.2 us
    reduce_scatter x1, waiting for transfers between devices, body(): coef_b = lax.psum_scatter(fock_lmo, 'col', scatter_dimension=0, tiled=True)  37.5 us
    all_to_all x1, waiting for transfers between devices, body(): tiles_a = lax.all_to_all(tiles_a, 'col', 0, 0, tiled=True)  35.7 us
    dot_general x1, matrix products, body(): jnp.dot(panel_fock, gathered, preferred_element_type=F32).astype(BF16)  23.4 us
    all_to_all x1, waiting for transfers between devices, body(): lax.all_to_all(tiles_b, 'row', 0, 0, tiled=True)  16.8 us
    all_to_all x1, waiting for transfers between devices, body(): lax.all_to_all(fc_b, 'row', 0, 0, tiled=True).reshape(dom_width, occ_width)  16.3 us
    unnamed x14, local copies, waits for them, and re-layouts  15.1 us
  transfers between devices with their start and end apart: 8, of which 5 were waited for; matrix products, arithmetic and copies ran while one was open for 19% of the time, Pallas kernels for 0%

commit v1 on v0

--- a/solution.py
+++ b/solution.py
@@ -53,7 +53,7 @@
     rows_a, tiles_a, fock_lmo = lax.optimization_barrier((rows_a, tiles_a, fock_lmo))
     coef_b = lax.psum_scatter(fock_lmo, "col", scatter_dimension=0, tiled=True)
     occ_term = jnp.einsum("ri,rj->ij", lmo_coef, coef_b, preferred_element_type=F32)
-    occ_b = lax.psum(occ_term, ("row", "col")).astype(BF16)
+    occ_b = lax.psum(lax.psum(occ_term, "row"), "col").astype(BF16)
     pres_o = lax.dynamic_index_in_dim(present, my_col, 0, keepdims=False)
     cset_o = lax.dynamic_index_in_dim(cset, my_col, 0, keepdims=False)
     pres_jk = lax.dynamic_index_in_dim(pres_o, my_row, 1, keepdims=False)

time: 484 us -> 505 us (1.043)
  waiting for transfers between devices: 172 us -> 238 us
  blocking collectives: 149 us -> 98.1 us
  starting transfers between devices: 38.6 us -> 44.2 us
    psum x0 -> x1, waiting for transfers between devices: none -> 63.9 us  [body(): occ_b = lax.psum(lax.psum(occ_term, 'row'), 'col').astype(BF16)]
    psum x1, blocking collectives: 149 us -> 98.1 us  [body(): occ_b = lax.psum(lax.psum(occ_term, 'row'), 'col').astype(BF16)]
    all_to_all x1, starting transfers between devices: 7.04 us -> 12.7 us  [body(): lax.all_to_all(fc_b, 'row', 0, 0, tiled=True).reshape(dom_width, occ_width)]
    unnamed x14 -> x12, local copies, waits for them, and re-layouts: 15.1 us -> 14.8 us
  transfers between devices with their start and end apart: 8 -> 9, of which waited for: 5 -> 6; matrix products, arithmetic and copies ran while one was open for 19% -> 18% of each run, Pallas kernels for 0% -> 0%
where the time goes in v1:
time: 505 us; the launch traced here: 503 us
  waiting for transfers between devices  238 us (47%)
  blocking collectives  98.1 us (19%)
  local copies, waits for them, and re-layouts  51.7 us (10%)
  matrix products  46.6 us (9%)
  starting transfers between devices  44.2 us (9%)
  between operations  13.9 us (3%)
  other arithmetic  10.9 us (2%)
    psum x1, blocking collectives, body(): occ_b = lax.psum(lax.psum(occ_term, 'row'), 'col').astype(BF16)  98.1 us
    all_to_all x1, waiting for transfers between devices, body(): rows_a = lax.all_to_all(rows_a, 'col', 0, 0, tiled=True)  65.2 us
    psum x1, waiting for transfers between devices, body(): occ_b = lax.psum(lax.psum(occ_term, 'row'), 'col').astype(BF16)  63.9 us
    reduce_scatter x1, waiting for transfers between devices, body(): coef_b = lax.psum_scatter(fock_lmo, 'col', scatter_dimension=0, tiled=True)  39.1 us
    all_to_all x1, waiting for transfers between devices, body(): tiles_a = lax.all_to_all(tiles_a, 'col', 0, 0, tiled=True)  35.8 us
    dot_general x1, matrix products, body(): jnp.dot(panel_fock, gathered, preferred_element_type=F32).astype(BF16)  23.4 us
    all_to_all x1, waiting for transfers between devices, body(): lax.all_to_all(tiles_b, 'row', 0, 0, tiled=True)  17.1 us
    all_to_all x1, waiting for transfers between devices, body(): lax.all_to_all(fc_b, 'row', 0, 0, tiled=True).reshape(dom_width, occ_width)  16.3 us
  transfers between devices with their start and end apart: 9, of which 6 were waited for; matrix products, arithmetic and copies ran while one was open for 18% of the time, Pallas kernels for 0%

profile of v1, /device:TPU:1, one launch (start us, length us, event | category | flops | bytes accessed | tf_op | source)
XLA Modules:
  0.0 503.5 jit_solution(2494622108919973887)
XLA Ops:
  12.3 3.6 gather_fusion.2
  15.9 8.5 %all-to-all-start = ((bf16[16,128,1536]{2,1,0:T(8,128)(2,1)}), bf16[16,128,1536]{2,1,0:T(8,128)(2,1)}, u32[]{:S(2)}, u32[]{:S(2)}) async-start(bf16[16,128,1536]{2,1,0:T(8,128)(2,1)} %gather_fusion.2), calls=%async_computation | async-start | bytes 12582912 | tf_op jit(solution)/shard_map/all_to_all | solution.py:48
  24.4 9.7 %copy.44 = bf16[512,8,16,128]{3,2,1,0:T(8,128)(2,1)S(1)} copy(bf16[512,8,16,128]{3,1,2,0:T(8,128)(2,1)} %bitcast.68) | data formatting | bytes 33554432
  34.1 8.2 %copy.33 = bf16[32,128,16,128]{3,1,2,0:T(8,128)(2,1)} copy(bf16[32,128,16,128]{3,2,1,0:T(8,128)(2,1)S(1)} %bitcast.65) | data formatting | bytes 33554432 | tf_op jit(solution)/shard_map/reshape;squeeze | solution.py:44
  42.5 9.0 %gather_fusion.1 = bf16[128,128,128]{2,1,0:T(8,128)(2,1)} fusion(bf16[32,128,16,128]{3,1,2,0:T(8,128)(2,1)} %copy.33, s32[128]{0:T(128)S(1)} %reshape.121), kind=kCustom, calls=%fused_computation.1 | custom fusion | bytes 8389632 | tf_op jit(solution)/shard_map/gather | solution.py:45
  51.5 65.2 %all-to-all-done = bf16[16,128,1536]{2,1,0:T(8,128)(2,1)} async-done(((bf16[16,128,1536]{2,1,0:T(8,128)(2,1)}), bf16[16,128,1536]{2,1,0:T(8,128)(2,1)}, u32[]{:S(2)}, u32[]{:S(2)}) %all-to-all-start) | async-done | bytes 6291488 | tf_op jit(solution)/shard_map/all_to_all | solution.py:48
  116.7 5.4 %all-to-all-start.1 = ((bf16[16,8,128,128]{3,2,1,0:T(8,128)(2,1)}), bf16[16,8,128,128]{3,2,1,0:T(8,128)(2,1)}, u32[]{:S(2)}, u32[]{:S(2)}) async-start(bf16[16,8,128,128]{3,2,1,0:T(8,128)(2,1)} %bitcast.69), calls=%async_computation.1 | async-start | bytes 8388608 | tf_op jit(solution)/shard_map/all_to_all | solution.py:50
  122.2 23.4 %fusion.2 = bf16[4096,1024]{1,0:T(8,128)(2,1)} fusion(bf16[2048,1024]{1,0:T(8,128)(2,1)} %all-gather.2.cloned.1.call-done, bf16[4096,1,2048]{2,0,1:T(8,128)(2,1)} %param.6), kind=kOutput, calls=%fused_computation.9 | convolution fusion | flops 17184063488 | bytes 29360128 | tf_op jit(solution)/shard_map/dot_general | solution.py:52
  145.6 35.8 %all-to-all-done.1 = bf16[16,8,128,128]{3,2,1,0:T(8,128)(2,1)} async-done(((bf16[16,8,128,128]{3,2,1,0:T(8,128)(2,1)}), bf16[16,8,128,128]{3,2,1,0:T(8,128)(2,1)}, u32[]{:S(2)}, u32[]{:S(2)}) %all-to-all-start.1) | async-done | bytes 4194336 | tf_op jit(solution)/shard_map/all_to_all | solution.py:50
  182.2 3.2 gather_fusion.5
  185.4 2.7 copy_select_fusion
  188.1 7.4 %all-to-all-start.4 = ((bf16[8,8,128,128]{3,1,2,0:T(8,128)(2,1)}), bf16[8,8,128,128]{3,1,2,0:T(8,128)(2,1)}, u32[]{:S(2)}, u32[]{:S(2)}) async-start(bf16[8,8,128,128]{3,1,2,0:T(8,128)(2,1)} %copy_select_fusion), calls=%async_computation.5 | async-start | bytes 4194304 | tf_op jit(solution)/shard_map/all_to_all | solution.py:69
  195.7 5.3 %gather_fusion.4 = bf16[8,128,1536]{2,1,0:T(8,128)(2,1)} fusion(bf16[16,128,1536]{2,1,0:T(8,128)(2,1)} %all-to-all-done, s32[1024]{0:T(1024)S(1)} %pad_clamp_fusion), kind=kCustom, calls=%fused_computation.4 | custom fusion | bytes 6291488 | tf_op jit(solution)/shard_map/jit(_take)/gather | solution.py:61
  201.0 3.9 broadcast_select_fusion
  204.9 17.1 %all-to-all-done.4 = bf16[8,8,128,128]{3,1,2,0:T(8,128)(2,1)} async-done(((bf16[8,8,128,128]{3,1,2,0:T(8,128)(2,1)}), bf16[8,8,128,128]{3,1,2,0:T(8,128)(2,1)}, u32[]{:S(2)}, u32[]{:S(2)}) %all-to-all-start.4) | async-done | bytes 2097184 | tf_op jit(solution)/shard_map/all_to_all | solution.py:69
  222.0 5.2 %all-to-all-start.3 = ((bf16[8,128,1536]{2,1,0:T(8,128)(2,1)}), bf16[8,128,1536]{2,1,0:T(8,128)(2,1)}, u32[]{:S(2)}, u32[]{:S(2)}) async-start(bf16[8,128,1536]{2,1,0:T(8,128)(2,1)} %broadcast_select_fusion), calls=%async_computation.4 | async-start | bytes 6291456 | tf_op jit(solution)/shard_map/all_to_all | solution.py:68
  227.2 39.1 %reduce-scatter.2.cloned.1.call-done = bf16[256,1024]{1,0:T(8,128)(2,1)} async-done(((bf16[4096,1024]{1,0:T(8,128)(2,1)}), bf16[256,1024]{1,0:T(8,128)(2,1)}) %reduce-scatter.2.cloned.1.call-update) | async-done | bytes 524304 | tf_op jit(solution)/shard_map/reduce_scatter | solution.py:54
  266.3 3.8 convolution_bitcast_fusion
  271.1 2.8 gather_fusion.3
  273.9 4.9 all-to-all-start.2
  278.8 63.9 %all-reduce.3.cloned.1.call-done = f32[1024,1024]{0,1:T(8,128)} async-done(((f32[1024,1024]{0,1:T(8,128)}), f32[1024,1024]{0,1:T(8,128)}) %all-reduce.3.cloned.1.call-update) | async-done | bytes 4194320 | tf_op jit(solution)/shard_map/psum | solution.py:56
  342.7 98.1 %all-reduce.4 = bf16[1024,1024]{0,1:T(8,128)(2,1)} all-reduce(f32[1024,1024]{0,1:T(8,128)} %all-reduce.3.cloned.1.call-done), channel_id=1, replica_groups=mesh['row'=8,'col'=16] {'col'}, use_global_device_ids=true, to_apply=%region_4.5 | all-reduce | flops 1048576 | bytes 6291456 | tf_op jit(solution)/shard_map/psum | solution.py:56
  440.8 2.9 gather_fusion.6
  443.7 1.5 broadcast_select_fusion.1
  445.2 12.7 %all-to-all-start.5 = ((bf16[8,128,1024]{2,1,0:T(8,128)(2,1)}), bf16[8,128,1024]{2,1,0:T(8,128)(2,1)}, u32[]{:S(2)}, u32[]{:S(2)}) async-start(bf16[8,128,1024]{2,1,0:T(8,128)(2,1)} %broadcast_select_fusion.1), calls=%async_computation.6 | async-start | bytes 4194304 | tf_op jit(solution)/shard_map/all_to_all | solution.py:77
  457.9 2.0 fusion.17
  460.9 2.9 fusion.11
  463.8 4.3 convolution_bitcast_fusion.1
  468.1 16.3 %all-to-all-done.5 = bf16[8,128,1024]{2,1,0:T(8,128)(2,1)} async-done(((bf16[8,128,1024]{2,1,0:T(8,128)(2,1)}), bf16[8,128,1024]{2,1,0:T(8,128)(2,1)}, u32[]{:S(2)}, u32[]{:S(2)}) %all-to-all-start.5) | async-done | bytes 2097184 | tf_op jit(solution)/shard_map/all_to_all | solution.py:77
  484.4 6.3 %convolution_convert_fusion = bf16[1024,512]{1,0:T(8,128)(2,1)S(1)} fusion(bf16[1,1,1024,512]{3,2,1,0:T(8,128)(2,1)S(1)} %copy-done, bf16[1024,1024]{1,0:T(8,128)(2,1)} %bitcast.22, bf16[1024,1024]{0,1:T(8,128)(2,1)} %all-reduce.4, bf16[1024,1536]{1,0:T(8,128)(2,1)} %bitcast.7), kind=kOutput, calls=%fused_computation.23 | convolution fusion | flops 3225944064 | bytes 8388608 | tf_op jit(solution)/shard_map/xm,xi->mi/dot_general | solution.py:88
  491.7 2.0 convolution_subtract_fusion.1
  493.7 2.0 fusion.16
  (44 shorter events, 10.6 us)
Async XLA Ops:
  7.2 450.8 %copy-start = (bf16[1,1,1024,512]{3,2,1,0:T(8,128)(2,1)S(1)}, bf16[1,1,1024,512]{3,2,1,0:T(8,128)(2,1)}, u32[]{:S(2)}) copy-start(bf16[1,1,1024,512]{3,2,1,0:T(8,128)(2,1)} %param.9) | copy-start | bytes 3145732
  7.2 115.0 %all-gather.2.cloned.1.call-start = ((), (), s32[]{:S(2)}) async-start(), calls=%async_computation.7 | async-start | bytes 4718592 | tf_op jit(solution)/shard_map/all_gather | solution.py:51
  15.9 100.8 %all-to-all-start = ((bf16[16,128,1536]{2,1,0:T(8,128)(2,1)}), bf16[16,128,1536]{2,1,0:T(8,128)(2,1)}, u32[]{:S(2)}, u32[]{:S(2)}) async-start(bf16[16,128,1536]{2,1,0:T(8,128)(2,1)} %gather_fusion.2), calls=%async_computation | async-start | bytes 12582912 | tf_op jit(solution)/shard_map/all_to_all | solution.py:48
  116.7 64.7 %all-to-all-start.1 = ((bf16[16,8,128,128]{3,2,1,0:T(8,128)(2,1)}), bf16[16,8,128,128]{3,2,1,0:T(8,128)(2,1)}, u32[]{:S(2)}, u32[]{:S(2)}) async-start(bf16[16,8,128,128]{3,2,1,0:T(8,128)(2,1)} %bitcast.69), calls=%async_computation.1 | async-start | bytes 8388608 | tf_op jit(solution)/shard_map/all_to_all | solution.py:50
  122.1 144.2 %reduce-scatter.2.cloned.1.call-start = ((), (), s32[]{:S(2)}) async-start(), calls=%async_computation.8 | async-start | bytes 8912896 | tf_op jit(solution)/shard_map/reduce_scatter | solution.py:54
  188.1 33.9 %all-to-all-start.4 = ((bf16[8,8,128,128]{3,1,2,0:T(8,128)(2,1)}), bf16[8,8,128,128]{3,1,2,0:T(8,128)(2,1)}, u32[]{:S(2)}, u32[]{:S(2)}) async-start(bf16[8,8,128,128]{3,1,2,0:T(8,128)(2,1)} %copy_select_fusion), calls=%async_computation.5 | async-start | bytes 4194304 | tf_op jit(solution)/shard_map/all_to_all | solution.py:69
  204.9 61.4 %copy-start.2 = (bf16[256,1024]{1,0:T(8,128)(2,1)S(1)}, bf16[256,1024]{1,0:T(8,128)(2,1)}, u32[]{:S(2)}) copy-start(bf16[256,1024]{1,0:T(8,128)(2,1)} %param.7) | copy-start | bytes 1572868
  222.0 51.9 %all-to-all-start.3 = ((bf16[8,128,1536]{2,1,0:T(8,128)(2,1)}), bf16[8,128,1536]{2,1,0:T(8,128)(2,1)}, u32[]{:S(2)}, u32[]{:S(2)}) async-start(bf16[8,128,1536]{2,1,0:T(8,128)(2,1)} %broadcast_select_fusion), calls=%async_computation.4 | async-start | bytes 6291456 | tf_op jit(solution)/shard_map/all_to_all | solution.py:68
  227.2 115.5 %all-reduce.3.cloned.1.call-start = ((), (), s32[]{:S(2)}) async-start(), calls=%async_computation.9 | async-start | bytes 8388608 | tf_op jit(solution)/shard_map/psum | solution.py:56
  270.1 1.0 copy-start.1
  273.9 166.9 %all-to-all-start.2 = ((bf16[16,128,1024]{2,1,0:T(8,128)(2,1)}), bf16[16,128,1024]{2,1,0:T(8,128)(2,1)}, u32[]{:S(2)}, u32[]{:S(2)}) async-start(bf16[16,128,1024]{2,1,0:T(8,128)(2,1)} %gather_fusion.3), calls=%async_computation.3 | async-start | bytes 8388608 | tf_op jit(solution)/shard_map/all_to_all | solution.py:73
  445.2 39.1 %all-to-all-start.5 = ((bf16[8,128,1024]{2,1,0:T(8,128)(2,1)}), bf16[8,128,1024]{2,1,0:T(8,128)(2,1)}, u32[]{:S(2)}, u32[]{:S(2)}) async-start(bf16[8,128,1024]{2,1,0:T(8,128)(2,1)} %broadcast_select_fusion.1), calls=%async_computation.6 | async-start | bytes 4194304 | tf_op jit(solution)/shard_map/all_to_all | solution.py:77
  490.7 1.0 copy-start.3
Sparse Core Ops, SparseCore 0:
  9.7 35.7 all-gather.1
  181.5 84.7 reduce-scatter.1
  270.2 72.4 all-reduce.2
